TPU v7x, 128 devices: a whole 4x4x4 slice. The times are simulated.
128 devices in a mesh: req: 16 (over y, x), head: 8 (over z, core).
Axes of the slice: x: 4, y: 4, z: 4, core: 2. Of those that a mesh axis runs over, the one named last changes fastest.
Arguments:
- hidden_in: bfloat16 [4864, 3072], P('req', 'head'), may hold values from -6 to 6
- dec_query: bfloat16 [768, 3072], P('req', 'head'), may hold values from -5.5 to 5.5
- dec_key: bfloat16 [768, 3072], P('req', 'head'), may hold values from -6 to 6
- dec_value: bfloat16 [768, 3072], P('req', 'head'), may hold values from -6 to 6
- pre_query: bfloat16 [4096, 3072], P('req', 'head'), may hold values from -5.5 to 5.5
- pre_key: bfloat16 [4096, 3072], P('req', 'head'), may hold values from -6 to 6
- pre_value: bfloat16 [4096, 3072], P('req', 'head'), may hold values from -6 to 6
- cache_key: bfloat16 [32, 2048, 3072], P('req', None, 'head'), may hold values from -5.5 to 5.5
- cache_value: bfloat16 [32, 2048, 3072], P('req', None, 'head'), may hold values from -6 to 6
- group_of: int32 [768, 1], replicated, may hold values from 0 to 31; in each aligned block of 768 rows (0 to 767, 768 to 1535, ...) at most 48 rows name the same one
- cache_length: int32 [32], P('req'), may hold values from 256 to 2048, as said below
- stretch_start: int32 [16], P('req'), may hold values from 256 to 2048, as said below
- row_owner: int32 [4864, 1], P('req'), may hold values from 0 to 15; in each aligned block of 304 rows (0 to 303, 304 to 607, ...) at most 40 rows name the same one
- out_weight: bfloat16 [3072, 3072], P('head'), may hold values from -0.109375 to 0.109375
- norm_gain: float32 [3072], replicated, may hold values from 0.1 to 1.9
- gate_weight: bfloat16 [3072, 4096], P(None, 'head'), may hold values from -0.109375 to 0.109375
- up_weight: bfloat16 [3072, 4096], P(None, 'head'), may hold values from -0.109375 to 0.109375
- down_weight: bfloat16 [4096, 3072], P('head'), may hold values from -0.09375 to 0.09375
Outputs:
- layer_out: bfloat16 [10240, 3072], P(('req', 'head'))
Inputs may be any that keep to these rules, and one draw needn't show every extreme that they name: `group_of`: at most 48 requests share a cache group, exactly 48 in some group; every group has a request. `cache_length`: some group has all 2048 rows valid. `stretch_start`: some stretch follows all 2048 cached rows. `row_owner`: among the 304 rows of one index of req at most 40 share an owner, exactly 40 on some index.
All inputs are finite; a program needn't handle non-finite values.
Results may differ from a plain program's by a relative error of at most 0.02.
Values may be sent and summed in bfloat16 or wider, within the bound.
No kernel may reach another device: no remote copies, remote signals or barrier semaphores. Data moves between devices by JAX's collectives and lax.ppermute only.
A program may use at most 128 MiB of HBM per device.

v0:
```python
import math
import jax
import jax.numpy as jnp
from jax import lax
from jax.sharding import PartitionSpec as P

HD = 96
CAP = 48
eps_norm = 1e-05


def head_split(matrix):
    return matrix.reshape(matrix.shape[0], matrix.shape[1] // HD, HD)


def softmax_rows(scores, allowed):
    masked = jnp.where(allowed, scores, -jnp.inf)
    highest = jnp.max(masked, axis=-1, keepdims=True)
    raised = jnp.exp(masked - highest)
    return (raised / jnp.sum(raised, axis=-1, keepdims=True)).astype(jnp.bfloat16)


def on_device(
    hidden_in,
    dec_query,
    dec_key,
    dec_value,
    pre_query,
    pre_key,
    pre_value,
    cache_key,
    cache_value,
    group_of,
    cache_length,
    stretch_start,
    row_owner,
    out_weight,
    norm_gain,
    gate_weight,
    up_weight,
    down_weight,
):
    factor = 1.0 / math.sqrt(HD)
    width_here = dec_query.shape[1]
    queries_all, keys_own, values_own = (
        lax.all_gather(dec_query, "req", axis=0, tiled=True),
        lax.all_gather(dec_key, "req", axis=0, tiled=True),
        lax.all_gather(dec_value, "req", axis=0, tiled=True),
    )
    groups_here = cache_key.shape[0]
    length_cache = cache_key.shape[1]
    first_group = lax.axis_index("req") * groups_here
    members = group_of[:, 0]
    wanted = first_group + jnp.arange(groups_here, dtype=jnp.int32)
    belongs = (members[None, :] == wanted[:, None]).astype(jnp.int32)
    ranking = jnp.cumsum(belongs, axis=1) - 1
    places = jnp.arange(CAP, dtype=jnp.int32)
    chosen = (belongs[:, None, :] == 1) & (ranking[:, None, :] == places[None, :, None])
    chooser = chosen.reshape(groups_here * CAP, members.shape[0])
    stacked_in = jnp.concatenate([queries_all, keys_own, values_own], axis=1)
    picked = jnp.dot(
        chooser.astype(jnp.bfloat16), stacked_in, preferred_element_type=jnp.float32
    ).astype(jnp.bfloat16)
    positions = jnp.arange(length_cache)
    results = []
    for group_pos in range(groups_here):
        rows_block = picked[group_pos * CAP : (group_pos + 1) * CAP]
        picked_q = head_split(rows_block[:, :width_here])
        picked_k = head_split(rows_block[:, width_here : 2 * width_here])
        picked_v = head_split(rows_block[:, 2 * width_here :])
        cache_scores = (
            jnp.einsum(
                "qhd,khd->hqk",
                picked_q,
                head_split(cache_key[group_pos]),
                preferred_element_type=jnp.float32,
            )
            * factor
        )
        own_scores = (
            jnp.sum(picked_q.astype(jnp.float32) * picked_k.astype(jnp.float32), axis=-1).T * factor
        )
        scores = jnp.concatenate([cache_scores, own_scores[:, :, None]], axis=-1)
        allowed = jnp.concatenate([positions < cache_length[group_pos], jnp.ones((1,), bool)])[
            None, None, :
        ]
        weights = softmax_rows(scores, allowed)
        blended = jnp.einsum(
            "hqk,khd->qhd",
            weights[:, :, :length_cache],
            head_split(cache_value[group_pos]),
            preferred_element_type=jnp.float32,
        )
        blended = blended + weights[:, :, length_cache].astype(jnp.float32).T[
            :, :, None
        ] * picked_v.astype(jnp.float32)
        results.append(blended.reshape(CAP, width_here))
    stacked = jnp.concatenate(results, axis=0)
    spread_back = jnp.dot(chooser.astype(jnp.float32).T, stacked, precision=lax.Precision.HIGHEST)
    dec_out = lax.psum_scatter(
        spread_back.astype(jnp.bfloat16), "req", scatter_dimension=0, tiled=True
    )
    stretch_len = pre_query.shape[0]
    key_rows = jnp.concatenate([cache_key[0], pre_key], axis=0)
    value_rows = jnp.concatenate([cache_value[0], pre_value], axis=0)
    columns = jnp.arange(length_cache + stretch_len)
    row_numbers = jnp.arange(stretch_len)
    allowed_pre = jnp.where(
        columns[None, :] < length_cache,
        columns[None, :] < stretch_start[0],
        columns[None, :] - length_cache <= row_numbers[:, None],
    )
    pre_scores = (
        jnp.einsum(
            "qhd,khd->hqk",
            head_split(pre_query),
            head_split(key_rows),
            preferred_element_type=jnp.float32,
        )
        * factor
    )
    pre_weights = softmax_rows(pre_scores, allowed_pre[None])
    pre_mixed = jnp.einsum(
        "hqk,khd->qhd", pre_weights, head_split(value_rows), preferred_element_type=jnp.float32
    )
    pre_out = pre_mixed.reshape(stretch_len, width_here).astype(jnp.bfloat16)
    attn_rows = jnp.concatenate([dec_out, pre_out], axis=0)
    projected = jnp.dot(attn_rows, out_weight, preferred_element_type=jnp.float32)
    col_start = lax.axis_index("head") * width_here
    own_cols = lax.dynamic_slice_in_dim(projected, col_start, width_here, 1) + hidden_in.astype(
        jnp.float32
    )
    contribution = lax.dynamic_update_slice_in_dim(projected, own_cols, col_start, 1)
    req_count = lax.axis_size("req")
    row_count = contribution.shape[0]
    slot_rows = 8 * ((2 * row_count + 8 * req_count - 1) // (8 * req_count))
    owners = row_owner[:, 0]
    onehot_owner = (owners[:, None] == jnp.arange(req_count, dtype=jnp.int32)[None, :]).astype(
        jnp.int32
    )
    before = jnp.sum((jnp.cumsum(onehot_owner, axis=0) - 1) * onehot_owner, axis=1)
    target = owners * slot_rows + before
    placing = (
        target[None, :] == jnp.arange(req_count * slot_rows, dtype=jnp.int32)[:, None]
    ).astype(jnp.bfloat16)
    residual = lax.psum(contribution.astype(jnp.bfloat16), "head")
    outgoing = jnp.dot(placing, residual, preferred_element_type=jnp.float32).astype(jnp.bfloat16)
    arrived = lax.all_to_all(outgoing, "req", split_axis=0, concat_axis=0, tiled=True)
    arrived_wide = arrived.astype(jnp.float32)
    squares = jnp.mean(jnp.square(arrived_wide), axis=-1, keepdims=True)
    normed = (arrived_wide * lax.rsqrt(squares + eps_norm) * norm_gain).astype(jnp.bfloat16)
    gate_act = jnp.dot(normed, gate_weight, preferred_element_type=jnp.float32)
    up_act = jnp.dot(normed, up_weight, preferred_element_type=jnp.float32)
    hidden = (jax.nn.silu(gate_act) * up_act).astype(jnp.bfloat16)
    rows_here = arrived.shape[0] // lax.axis_size("head")
    down_sum = lax.psum_scatter(
        jnp.dot(hidden, down_weight, preferred_element_type=jnp.float32).astype(jnp.bfloat16),
        "head",
        scatter_dimension=0,
        tiled=True,
    ).astype(jnp.float32)
    own_rows = lax.dynamic_slice_in_dim(
        arrived_wide, lax.axis_index("head") * rows_here, rows_here, 0
    )
    return (own_rows + down_sum).astype(jnp.bfloat16)


def solution(mesh):
    placed = (
        P("req", "head"),
        P("req", "head"),
        P("req", "head"),
        P("req", "head"),
        P("req", "head"),
        P("req", "head"),
        P("req", "head"),
        P("req", None, "head"),
        P("req", None, "head"),
        P(),
        P("req"),
        P("req"),
        P("req", None),
        P("head", None),
        P(),
        P(None, "head"),
        P(None, "head"),
        P("head", None),
    )
    return jax.shard_map(
        on_device, mesh=mesh, in_specs=placed, out_specs=P(("req", "head"), None), check_vma=False
    )
```

profile of v0, /device:TPU:0, one launch (start us, length us, event | category | flops | bytes accessed | tf_op | source)
XLA Modules:
  0.0 390.3 jit_solution(7005297331430344854)
XLA Ops:
  6.6 1.5 fusion.83
  8.8 1.3 iota_compare_fusion.7
  11.9 24.6 %all_gather.9 = bf16[768,384]{1,0:T(8,128)(2,1)S(1)} all-gather(bf16[48,384]{1,0:T(8,128)(2,1)} %param.19), channel_id=1, replica_groups=mesh['req'=16,'head'=8] {'req'}, dimensions={0}, use_global_device_ids=true | all-gather | bytes 626688 | tf_op jit(solution)/shard_map/all_gather | solution.py:46
  36.5 23.5 %all_gather.10 = bf16[768,384]{1,0:T(8,128)(2,1)S(1)} all-gather(bf16[48,384]{1,0:T(8,128)(2,1)} %param.20), channel_id=1, replica_groups=mesh['req'=16,'head'=8] {'req'}, dimensions={0}, use_global_device_ids=true | all-gather | bytes 626688 | tf_op jit(solution)/shard_map/all_gather | solution.py:47
  60.0 21.9 %all_gather.11 = bf16[768,384]{1,0:T(8,128)(2,1)S(1)} all-gather(bf16[48,384]{1,0:T(8,128)(2,1)} %param.21), channel_id=1, replica_groups=mesh['req'=16,'head'=8] {'req'}, dimensions={0}, use_global_device_ids=true | all-gather | bytes 626688 | tf_op jit(solution)/shard_map/all_gather | solution.py:48
  89.7 3.9 fusion.81
  93.5 2.6 copy.77
  96.2 1.8 convolution_multiply_fusion
  99.7 2.6 copy.70
  102.3 1.8 convolution_multiply_fusion.1
  106.2 1.9 fusion.82
  108.2 2.6 copy.81
  110.8 2.3 fusion.31
  113.3 2.7 copy.74
  115.9 2.3 fusion.32
  118.5 1.5 convolution_convert_fusion.3
  123.6 1.7 copy.84
  125.4 3.8 fusion.12
  129.2 4.9 %fusion.84 = f32[4,256]{1,0:T(4,128)S(1)} fusion(pred[256,2304]{0,1:T(8,128)(4,1)} %fusion.12, bf16[256,4,96]{0,2,1:T(8,128)(2,1)S(1)} %bitcast.97, bf16[256,4,96]{0,2,1:T(8,128)(2,1)S(1)} %bitcast.99, bf16[2048,4,96]{0,2,1:T(8,128)(2,1)} %bitcast.90), kind=kOutput, calls=%fused_computation.125 | convolution fusion | flops 465963264 | bytes 2560000 | tf_op jit(solution)/shard_map/sub | solution.py:19
  134.0 7.6 %fusion.28 = bf16[4,96,256]{2,1,0:T(8,128)(2,1)} fusion(f32[4,256]{1,0:T(4,128)S(1)} %fusion.84, bf16[256,4,96]{0,2,1:T(8,128)(2,1)} %bitcast.101, bf16[2048,4,96]{0,2,1:T(8,128)(2,1)} %bitcast.93, pred[256,2304]{0,1:T(8,128)(4,1)} %fusion.12, bf16[256,4,96]{0,2,1:T(8,128)(2,1)S(1)} %bitcast.98, bf16[256,4,96]{0,2,1:T(8,128)(2,1)S(1)} %bitcast.100, ...), kind=kOutput, calls=%fused_computation.45 | convolution fusion | flops 924945664 | bytes 4526080 | tf_op jit(solution)/shard_map/hqk,khd->qhd/dot_general | solution.py:123
  141.7 51.4 %reduce-scatter.7.cloned.1.call-done = bf16[48,384]{1,0:T(8,128)(2,1)} async-done(((bf16[768,384]{1,0:T(8,128)(2,1)}), bf16[48,384]{1,0:T(8,128)(2,1)}) %reduce-scatter.7.cloned.1.call-update) | async-done | bytes 36880
  193.9 3.1 fusion.44
  197.1 1.5 convert_element_type.133
  200.2 63.4 %all-reduce.4.cloned.1.call-done = bf16[304,3072]{1,0:T(8,128)(2,1)} async-done(((bf16[304,3072]{1,0:T(8,128)(2,1)}), bf16[304,3072]{1,0:T(8,128)(2,1)}) %all-reduce.4.cloned.1.call-update) | async-done | bytes 1867792 | tf_op jit(solution)/shard_map/psum | solution.py:146
  263.6 3.7 convolution_convert_fusion.1
  267.3 52.8 %all_to_all.9 = bf16[16,40,3072]{2,1,0:T(8,128)(2,1)S(1)} all-to-all(bf16[16,40,3072]{2,1,0:T(8,128)(2,1)S(1)} %bitcast.96), channel_id=1, replica_groups=mesh['req'=16,'head'=8] {'req'}, dimensions={0} | all-to-all | bytes 7864320 | tf_op jit(solution)/shard_map/all_to_all | solution.py:148
  322.2 6.9 %multiply_convert_fusion = (bf16[640,3072]{1,0:T(8,128)(2,1)S(1)}, f32[16,40,3072]{2,1,0:T(8,128)}) fusion(f32[3072]{0:T(1024)S(1)} %copy-done.10, f32[640]{0:T(1024)S(1)} %rsqrt.12, bf16[16,40,3072]{2,1,0:T(8,128)(2,1)} %copy-done.1), kind=kLoop, calls=%fused_computation.7 | loop fusion | flops 7864320 | bytes 15743488 | tf_op jit(solution)/shard_map/convert_element_type | solution.py:151
  329.1 2.0 copy-done.2
  331.1 3.2 fusion.89
  334.4 9.7 %convolution_convert_fusion = bf16[640,3072]{1,0:T(8,128)(2,1)} fusion(bf16[512,3072]{1,0:T(8,128)(2,1)S(1)} %copy-done, bf16[640,3072]{1,0:T(8,128)(2,1)} %copy-done.2, bf16[3072,512]{1,0:T(8,128)(2,1)} %param.34, f32[640,512]{1,0:T(8,128)} %fusion.89), kind=kOutput, calls=%fused_computation.9 | convolution fusion | flops 4030464000 | bytes 15466496 | tf_op jit(solution)/shard_map/dot_general | solution.py:157
  344.1 37.5 %reduce-scatter.5.cloned.1.call-done = bf16[80,3072]{1,0:T(8,128)(2,1)} async-done(((bf16[640,3072]{1,0:T(8,128)(2,1)}), bf16[80,3072]{1,0:T(8,128)(2,1)}) %reduce-scatter.5.cloned.1.call-update) | async-done | bytes 491536 | tf_op jit(solution)/shard_map/reduce_scatter | solution.py:156
  381.6 2.2 add_convert_fusion
  (89 shorter events, 22.0 us)
Async XLA Ops:
  6.5 327.8 %copy-start = (bf16[512,3072]{1,0:T(8,128)(2,1)S(1)}, bf16[512,3072]{1,0:T(8,128)(2,1)}, u32[]{:S(2)}) copy-start(bf16[512,3072]{1,0:T(8,128)(2,1)} %param.35) | copy-start | bytes 9437188
  6.5 186.5 %reduce-scatter.7.cloned.1.call-start = ((), (), s32[]{:S(2)}) async-start(), calls=%async_computation.5 | async-start | bytes 626688
  82.1 0.6 copy-start.6
  96.2 1.8 copy-start.11
  96.2 1.8 copy-start.9
  98.7 0.9 copy-start.3
  104.0 2.2 copy-start.5
  104.7 0.9 copy-start.4
  115.9 2.5 copy-start.7
  115.9 4.9 %copy-start.12 = (s32[304,1]{0,1:T(1,128)S(1)}, s32[304,1]{0,1:T(1,128)}, u32[]{:S(2)}) copy-start(s32[304,1]{0,1:T(1,128)} %param.30) | copy-start | bytes 3652
  120.0 143.6 %all-reduce.4.cloned.1.call-start = ((), (), s32[]{:S(2)}) async-start(), calls=%async_computation.3 | async-start | bytes 3735552 | tf_op jit(solution)/shard_map/psum | solution.py:146
  193.9 3.1 copy-start.8
  198.6 182.9 %reduce-scatter.5.cloned.1.call-start = ((), (), s32[]{:S(2)}) async-start(), calls=%async_computation.4 | async-start | bytes 4423680 | tf_op jit(solution)/shard_map/reduce_scatter | solution.py:156
  320.1 2.0 copy-start.1
  320.1 2.1 copy-start.10
  322.2 8.9 %copy-start.13 = (bf16[3072,512]{1,0:T(8,128)(2,1)S(1)}, bf16[3072,512]{1,0:T(8,128)(2,1)}, u32[]{:S(2)}) copy-start(bf16[3072,512]{1,0:T(8,128)(2,1)} %param.33) | copy-start | bytes 9437188
  329.1 2.0 copy-start.2
Sparse Core Ops, SparseCore 0:
  120.1 72.9 reduce-scatter.6
  198.8 64.7 all-reduce.3
  344.2 37.3 reduce-scatter.4
where the time goes:
time: 392 us; the launch traced here: 390 us
  waiting for transfers between devices  152 us (39%)
  blocking collectives  123 us (31%)
  matrix products  42.3 us (11%)
  local copies, waits for them, and re-layouts  34.5 us (9%)
  other arithmetic  23.7 us (6%)
  between operations  14.1 us (4%)
    psum x1, waiting for transfers between devices, on_device(): residual = lax.psum(contribution.astype(jnp.bfloat16), 'head')  63.4 us
    all_to_all x1, blocking collectives, on_device(): lax.all_to_all(outgoing, 'req', split_axis=0, concat_axis=0, tiled=True)  52.8 us
    unnamed x4, waiting for transfers between devices  51.4 us
    reduce_scatter x1, waiting for transfers between devices, on_device(): lax.psum_scatter(jnp.dot(hidden, down_weight, preferred_element_type=jnp....  37.5 us
    all_gather x1, blocking collectives, on_device(): lax.all_gather(dec_query, 'req', axis=0, tiled=True)  24.6 us
    all_gather x1, blocking collectives, on_device(): lax.all_gather(dec_key, 'req', axis=0, tiled=True)  23.5 us
    all_gather x1, blocking collectives, on_device(): lax.all_gather(dec_value, 'req', axis=0, tiled=True)  21.9 us
    dot_general x1, matrix products, on_device(): jnp.dot(hidden, down_weight, preferred_element_type=jnp.float32)  9.69 us
  transfers between devices with their start and end apart: 3, of which 3 were waited for; matrix products, arithmetic and copies ran while one was open for 6% of the time, Pallas kernels for 0%

commit v1 on v0

--- a/solution.py
+++ b/solution.py
@@ -7,6 +7,27 @@
 HD = 96
 CAP = 48
 eps_norm = 1e-05
+
+
+def teams_pass(t0):
+    moved, then, block_last = (lax.axis_size("req"), lax.axis_index("req"), t0.shape[0])
+    made = tuple((dev_j * moved if b == 0 else dev_j for b, dev_j in enumerate(t0.shape)))
+    formed = lax.dynamic_update_slice_in_dim(
+        jnp.zeros(made, t0.dtype), t0, then * block_last, axis=0
+    )
+    high = everything = t0
+    for q in range(1, moved // 2 + 1):
+        high = lax.ppermute(high, "req", tuple(((b, (b + 1) % moved) for b in range(moved))))
+        formed = lax.dynamic_update_slice_in_dim(
+            formed, high, (then - q) % moved * block_last, axis=0
+        )
+        if 2 * q < moved:
+            aux = tuple(((b, (b - 1) % moved) for b in range(moved)))
+            everything = lax.ppermute(everything, "req", aux)
+            formed = lax.dynamic_update_slice_in_dim(
+                formed, everything, (then + q) % moved * block_last, axis=0
+            )
+    return formed
 
 
 def head_split(matrix):
@@ -43,7 +64,7 @@
     factor = 1.0 / math.sqrt(HD)
     width_here = dec_query.shape[1]
     queries_all, keys_own, values_own = (
-        lax.all_gather(dec_query, "req", axis=0, tiled=True),
+        teams_pass(dec_query),
         lax.all_gather(dec_key, "req", axis=0, tiled=True),
         lax.all_gather(dec_value, "req", axis=0, tiled=True),
     )

time: 392 us -> 440 us (1.12)
  starting transfers between devices: 0.49 us -> 36.3 us
  blocking collectives: 123 us -> 105 us
  waiting for transfers between devices: 152 us -> 169 us
  local copies, waits for them, and re-layouts: 34.5 us -> 48.3 us
    ppermute x0 -> x15, starting transfers between devices: none -> 36 us  [the longest x7 36 us: teams_pass(): everything = lax.ppermute(everything, 'req', aux)]
    all_gather x1 -> x0, blocking collectives: 24.6 us -> none  [on_device(): lax.all_gather(dec_query, 'req', axis=0, tiled=True)]
    ppermute x0 -> x15, waiting for transfers between devices: none -> 13.7 us  [the longest x8 12.1 us: teams_pass(): lax.ppermute(high, 'req', tuple(((b, (b + 1) % moved) for b in range(move...]
    dynamic_update_slice x0 -> x16, local copies, waits for them, and re-layouts: none -> 12.1 us  [the longest x8 5.7 us: teams_pass(): lax.dynamic_update_slice_in_dim(formed, high, (then - q) % moved * block_...]
    unnamed x32 -> x52, local copies, waits for them, and re-layouts: 9.55 us -> 9.68 us
  transfers between devices with their start and end apart: 3 -> 18, of which waited for: 3 -> 9; matrix products, arithmetic and copies ran while one was open for 6% -> 13% of each run, Pallas kernels for 0% -> 0%
where the time goes in v1:
time: 440 us; the launch traced here: 439 us
  waiting for transfers between devices  169 us (38%)
  blocking collectives  105 us (24%)
  local copies, waits for them, and re-layouts  48.3 us (11%)
  matrix products  40.8 us (9%)
  starting transfers between devices  36.3 us (8%)
  other arithmetic  25.3 us (6%)
  between operations  14.2 us (3%)
    psum x1, waiting for transfers between devices, on_device(): residual = lax.psum(contribution.astype(jnp.bfloat16), 'head')  63.3 us
    unnamed x4, waiting for transfers between devices  54.9 us
    all_to_all x1, blocking collectives, on_device(): lax.all_to_all(outgoing, 'req', split_axis=0, concat_axis=0, tiled=True)  52.8 us
    reduce_scatter x1, waiting for transfers between devices, on_device(): lax.psum_scatter(jnp.dot(hidden, down_weight, preferred_element_type=jnp....  37.5 us
    ppermute x7, starting transfers between devices, teams_pass(): everything = lax.ppermute(everything, 'req', aux)  36 us
    all_gather x1, blocking collectives, on_device(): lax.all_gather(dec_key, 'req', axis=0, tiled=True)  27.1 us
    all_gather x1, blocking collectives, on_device(): lax.all_gather(dec_value, 'req', axis=0, tiled=True)  24.8 us
    ppermute x8, waiting for transfers between devices, teams_pass(): lax.ppermute(high, 'req', tuple(((b, (b + 1) % moved) for b in range(move...  12.1 us
  transfers between devices with their start and end apart: 18, of which 9 were waited for; matrix products, arithmetic and copies ran while one was open for 13% of the time, Pallas kernels for 0%

profile of v1, /device:TPU:0, one launch (start us, length us, event | category | flops | bytes accessed | tf_op | source)
XLA Modules:
  0.0 439.1 jit_solution(12094074091192103739)
XLA Ops:
  6.5 5.3 %collective-permute-start.1 = (bf16[48,384]{1,0:T(8,128)(2,1)}, bf16[48,384]{1,0:T(8,128)(2,1)}, u32[]{:S(2)}, u32[]{:S(2)}) collective-permute-start(bf16[48,384]{1,0:T(8,128)(2,1)} %param.19), channel_id=1, source_target_pairs={{0,120},{8,0},{16,8},{24,16},{32,24},{40,32},{48,40},{56,48},{64,5... | collective-permute-start | bytes 110600 | tf_op jit(solution)/shard_map/ppermute | solution.py:26
  19.0 27.1 %all_gather.6 = bf16[768,384]{1,0:T(8,128)(2,1)} all-gather(bf16[48,384]{1,0:T(8,128)(2,1)} %param.20), channel_id=1, replica_groups=mesh['req'=16,'head'=8] {'req'}, dimensions={0}, use_global_device_ids=true | all-gather | bytes 626688 | tf_op jit(solution)/shard_map/all_gather | solution.py:68
  46.0 24.8 %all_gather.7 = bf16[768,384]{1,0:T(8,128)(2,1)} all-gather(bf16[48,384]{1,0:T(8,128)(2,1)} %param.21), channel_id=1, replica_groups=mesh['req'=16,'head'=8] {'req'}, dimensions={0}, use_global_device_ids=true | all-gather | bytes 626688 | tf_op jit(solution)/shard_map/all_gather | solution.py:69
  70.9 4.0 fusion.81
  74.9 1.9 fusion.82
  85.7 2.6 copy.77
  88.4 2.6 copy.70
  90.9 2.6 copy.81
  93.6 2.7 copy.74
  96.4 2.7 collective-permute-start.3
  101.9 5.3 %collective-permute-start.5 = (bf16[48,384]{1,0:T(8,128)(2,1)S(1)}, bf16[48,384]{1,0:T(8,128)(2,1)S(1)}, u32[]{:S(2)}, u32[]{:S(2)}) collective-permute-start(bf16[48,384]{1,0:T(8,128)(2,1)S(1)} %collective-permute-done.3), channel_id=1, source_target_pairs={{0,120},{8,0},{16,8},{24,16},{32,24},{40,32},{48,40},{56,48},{64,5... | collective-permute-start | bytes 110600 | tf_op jit(solution)/shard_map/ppermute | solution.py:26
  108.9 5.7 %collective-permute-start.7 = (bf16[48,384]{1,0:T(8,128)(2,1)S(1)}, bf16[48,384]{1,0:T(8,128)(2,1)S(1)}, u32[]{:S(2)}, u32[]{:S(2)}) collective-permute-start(bf16[48,384]{1,0:T(8,128)(2,1)S(1)} %collective-permute-done.5), channel_id=1, source_target_pairs={{0,120},{8,0},{16,8},{24,16},{32,24},{40,32},{48,40},{56,48},{64,5... | collective-permute-start | bytes 110600 | tf_op jit(solution)/shard_map/ppermute | solution.py:26
  116.2 5.6 %collective-permute-start.9 = (bf16[48,384]{1,0:T(8,128)(2,1)S(1)}, bf16[48,384]{1,0:T(8,128)(2,1)S(1)}, u32[]{:S(2)}, u32[]{:S(2)}) collective-permute-start(bf16[48,384]{1,0:T(8,128)(2,1)S(1)} %collective-permute-done.7), channel_id=1, source_target_pairs={{0,120},{8,0},{16,8},{24,16},{32,24},{40,32},{48,40},{56,48},{64,5... | collective-permute-start | bytes 110600 | tf_op jit(solution)/shard_map/ppermute | solution.py:26
  123.5 5.6 %collective-permute-start.11 = (bf16[48,384]{1,0:T(8,128)(2,1)S(1)}, bf16[48,384]{1,0:T(8,128)(2,1)S(1)}, u32[]{:S(2)}, u32[]{:S(2)}) collective-permute-start(bf16[48,384]{1,0:T(8,128)(2,1)S(1)} %collective-permute-done.9), channel_id=1, source_target_pairs={{0,120},{8,0},{16,8},{24,16},{32,24},{40,32},{48,40},{56,48},{64,5... | collective-permute-start | bytes 110600 | tf_op jit(solution)/shard_map/ppermute | solution.py:26
  130.8 5.6 %collective-permute-start.13 = (bf16[48,384]{1,0:T(8,128)(2,1)S(1)}, bf16[48,384]{1,0:T(8,128)(2,1)S(1)}, u32[]{:S(2)}, u32[]{:S(2)}) collective-permute-start(bf16[48,384]{1,0:T(8,128)(2,1)S(1)} %collective-permute-done.11), channel_id=1, source_target_pairs={{0,120},{8,0},{16,8},{24,16},{32,24},{40,32},{48,40},{56,48},{64,5... | collective-permute-start | bytes 110600 | tf_op jit(solution)/shard_map/ppermute | solution.py:26
  137.7 6.0 %collective-permute-done.12 = bf16[48,384]{1,0:T(8,128)(2,1)S(1)} collective-permute-done((bf16[48,384]{1,0:T(8,128)(2,1)S(1)}, bf16[48,384]{1,0:T(8,128)(2,1)S(1)}, u32[]{:S(2)}, u32[]{:S(2)}) %collective-permute-start.12) | collective-permute-done | bytes 36896 | tf_op jit(solution)/shard_map/ppermute | solution.py:20
  144.9 6.0 %collective-permute-done.14 = bf16[48,384]{1,0:T(8,128)(2,1)S(1)} collective-permute-done((bf16[48,384]{1,0:T(8,128)(2,1)S(1)}, bf16[48,384]{1,0:T(8,128)(2,1)S(1)}, u32[]{:S(2)}, u32[]{:S(2)}) %collective-permute-start.14) | collective-permute-done | bytes 36896 | tf_op jit(solution)/shard_map/ppermute | solution.py:20
  167.6 2.3 fusion.32
  171.7 2.7 fusion.12
  174.4 5.0 %fusion.84 = f32[4,256]{1,0:T(4,128)S(1)} fusion(pred[256,2304]{0,1:T(8,128)(4,1)} %fusion.12, bf16[256,4,96]{0,2,1:T(8,128)(2,1)} %bitcast.97, bf16[256,4,96]{0,2,1:T(8,128)(2,1)} %bitcast.99, bf16[2048,4,96]{0,2,1:T(8,128)(2,1)} %bitcast.89), kind=kOutput, calls=%fused_computation.141 | convolution fusion | flops 465963264 | bytes 2560000 | tf_op jit(solution)/shard_map/sub | solution.py:40
  179.5 7.6 %fusion.28 = bf16[4,96,256]{2,1,0:T(8,128)(2,1)} fusion(f32[4,256]{1,0:T(4,128)S(1)} %fusion.84, bf16[256,4,96]{0,2,1:T(8,128)(2,1)} %bitcast.101, bf16[2048,4,96]{0,2,1:T(8,128)(2,1)} %bitcast.93, pred[256,2304]{0,1:T(8,128)(4,1)} %fusion.12, bf16[256,4,96]{0,2,1:T(8,128)(2,1)S(1)} %bitcast.98, bf16[256,4,96]{0,2,1:T(8,128)(2,1)S(1)} %bitcast.100, ...), kind=kOutput, calls=%fused_computation.45 | convolution fusion | flops 924945664 | bytes 4526080 | tf_op jit(solution)/shard_map/hqk,khd->qhd/dot_general | solution.py:144
  187.0 54.9 %reduce-scatter.7.cloned.1.call-done = bf16[48,384]{1,0:T(8,128)(2,1)} async-done(((bf16[768,384]{1,0:T(8,128)(2,1)}), bf16[48,384]{1,0:T(8,128)(2,1)}) %reduce-scatter.7.cloned.1.call-update) | async-done | bytes 36880
  242.8 3.1 fusion.44
  249.1 63.3 %all-reduce.4.cloned.1.call-done = bf16[304,3072]{1,0:T(8,128)(2,1)} async-done(((bf16[304,3072]{1,0:T(8,128)(2,1)}), bf16[304,3072]{1,0:T(8,128)(2,1)}) %all-reduce.4.cloned.1.call-update) | async-done | bytes 1867792 | tf_op jit(solution)/shard_map/psum | solution.py:167
  312.4 3.7 convolution_convert_fusion.1
  316.1 52.8 %all_to_all.9 = bf16[16,40,3072]{2,1,0:T(8,128)(2,1)S(1)} all-to-all(bf16[16,40,3072]{2,1,0:T(8,128)(2,1)S(1)} %bitcast.96), channel_id=1, replica_groups=mesh['req'=16,'head'=8] {'req'}, dimensions={0} | all-to-all | bytes 7864320 | tf_op jit(solution)/shard_map/all_to_all | solution.py:169
  371.0 6.9 %multiply_convert_fusion = (bf16[640,3072]{1,0:T(8,128)(2,1)S(1)}, f32[16,40,3072]{2,1,0:T(8,128)}) fusion(f32[3072]{0:T(1024)S(1)} %copy-done.17, f32[640]{0:T(1024)S(1)} %rsqrt.12, bf16[16,40,3072]{2,1,0:T(8,128)(2,1)} %copy-done.1), kind=kLoop, calls=%fused_computation.7 | loop fusion | flops 7864320 | bytes 15743488 | tf_op jit(solution)/shard_map/convert_element_type | solution.py:172
  377.9 2.0 copy-done.4
  379.9 3.2 fusion.89
  383.2 9.7 %convolution_convert_fusion = bf16[640,3072]{1,0:T(8,128)(2,1)} fusion(bf16[512,3072]{1,0:T(8,128)(2,1)S(1)} %copy-done, bf16[640,3072]{1,0:T(8,128)(2,1)} %copy-done.4, bf16[3072,512]{1,0:T(8,128)(2,1)} %param.34, f32[640,512]{1,0:T(8,128)} %fusion.89), kind=kOutput, calls=%fused_computation.9 | convolution fusion | flops 4030464000 | bytes 15466496 | tf_op jit(solution)/shard_map/dot_general | solution.py:178
  392.9 37.5 %reduce-scatter.5.cloned.1.call-done = bf16[80,3072]{1,0:T(8,128)(2,1)} async-done(((bf16[640,3072]{1,0:T(8,128)(2,1)}), bf16[80,3072]{1,0:T(8,128)(2,1)}) %reduce-scatter.5.cloned.1.call-update) | async-done | bytes 491536 | tf_op jit(solution)/shard_map/reduce_scatter | solution.py:177
  430.4 2.2 add_convert_fusion
  (155 shorter events, 51.5 us)
Async XLA Ops:
  6.5 376.6 %copy-start = (bf16[512,3072]{1,0:T(8,128)(2,1)S(1)}, bf16[512,3072]{1,0:T(8,128)(2,1)}, u32[]{:S(2)}) copy-start(bf16[512,3072]{1,0:T(8,128)(2,1)} %param.35) | copy-start | bytes 9437188
  6.5 235.4 %reduce-scatter.7.cloned.1.call-start = ((), (), s32[]{:S(2)}) async-start(), calls=%async_computation.5 | async-start | bytes 626688
  6.5 89.9 %collective-permute-start.1 = (bf16[48,384]{1,0:T(8,128)(2,1)}, bf16[48,384]{1,0:T(8,128)(2,1)}, u32[]{:S(2)}, u32[]{:S(2)}) collective-permute-start(bf16[48,384]{1,0:T(8,128)(2,1)} %param.19), channel_id=1, source_target_pairs={{0,120},{8,0},{16,8},{24,16},{32,24},{40,32},{48,40},{56,48},{64,5... | collective-permute-start | bytes 110600 | tf_op jit(solution)/shard_map/ppermute | solution.py:26
  11.9 87.3 %collective-permute-start = (bf16[48,384]{1,0:T(8,128)(2,1)}, bf16[48,384]{1,0:T(8,128)(2,1)}, u32[]{:S(2)}, u32[]{:S(2)}) collective-permute-start(bf16[48,384]{1,0:T(8,128)(2,1)} %param.19), channel_id=1, source_target_pairs={{0,8},{8,16},{16,24},{24,32},{32,40},{40,48},{48,56},{56,64},{64,7... | collective-permute-start | bytes 110600 | tf_op jit(solution)/shard_map/ppermute | solution.py:20
  70.9 4.0 copy-start.6
  74.9 7.5 %copy-start.10 = (bf16[256,384]{1,0:T(8,128)(2,1)S(1)}, bf16[256,384]{1,0:T(8,128)(2,1)}, u32[]{:S(2)}) copy-start(bf16[256,384]{1,0:T(8,128)(2,1)} %param.22) | copy-start | bytes 589828
  74.9 8.3 %copy-start.11 = (bf16[256,384]{1,0:T(8,128)(2,1)S(1)}, bf16[256,384]{1,0:T(8,128)(2,1)}, u32[]{:S(2)}) copy-start(bf16[256,384]{1,0:T(8,128)(2,1)} %param.23) | copy-start | bytes 589828
  96.4 57.1 %copy-start.7 = (pred[96,768]{1,0:T(32,128)(4,1)}, pred[96,768]{1,0:T(32,128)(4,1)S(1)}, u32[]{:S(2)}) copy-start(pred[96,768]{1,0:T(32,128)(4,1)S(1)} %fusion.48) | copy-start | bytes 221188
  96.4 5.5 %collective-permute-start.3 = (bf16[48,384]{1,0:T(8,128)(2,1)}, bf16[48,384]{1,0:T(8,128)(2,1)S(1)}, u32[]{:S(2)}, u32[]{:S(2)}) collective-permute-start(bf16[48,384]{1,0:T(8,128)(2,1)} %collective-permute-done.1), channel_id=1, source_target_pairs={{0,120},{8,0},{16,8},{24,16},{32,24},{40,32},{48,40},{56,48},{64,5... | collective-permute-start | bytes 110600 | tf_op jit(solution)/shard_map/ppermute | solution.py:26
  99.1 8.1 %collective-permute-start.2 = (bf16[48,384]{1,0:T(8,128)(2,1)}, bf16[48,384]{1,0:T(8,128)(2,1)S(1)}, u32[]{:S(2)}, u32[]{:S(2)}) collective-permute-start(bf16[48,384]{1,0:T(8,128)(2,1)} %collective-permute-done), channel_id=1, source_target_pairs={{0,8},{8,16},{16,24},{24,32},{32,40},{40,48},{48,56},{56,64},{64,7... | collective-permute-start | bytes 110600 | tf_op jit(solution)/shard_map/ppermute | solution.py:20
  101.9 7.0 %collective-permute-start.5 = (bf16[48,384]{1,0:T(8,128)(2,1)S(1)}, bf16[48,384]{1,0:T(8,128)(2,1)S(1)}, u32[]{:S(2)}, u32[]{:S(2)}) collective-permute-start(bf16[48,384]{1,0:T(8,128)(2,1)S(1)} %collective-permute-done.3), channel_id=1, source_target_pairs={{0,120},{8,0},{16,8},{24,16},{32,24},{40,32},{48,40},{56,48},{64,5... | collective-permute-start | bytes 110600 | tf_op jit(solution)/shard_map/ppermute | solution.py:26
  107.3 7.3 %collective-permute-start.4 = (bf16[48,384]{1,0:T(8,128)(2,1)S(1)}, bf16[48,384]{1,0:T(8,128)(2,1)S(1)}, u32[]{:S(2)}, u32[]{:S(2)}) collective-permute-start(bf16[48,384]{1,0:T(8,128)(2,1)S(1)} %collective-permute-done.2), channel_id=1, source_target_pairs={{0,8},{8,16},{16,24},{24,32},{32,40},{40,48},{48,56},{56,64},{64,7... | collective-permute-start | bytes 110600 | tf_op jit(solution)/shard_map/ppermute | solution.py:20
  108.9 7.3 %collective-permute-start.7 = (bf16[48,384]{1,0:T(8,128)(2,1)S(1)}, bf16[48,384]{1,0:T(8,128)(2,1)S(1)}, u32[]{:S(2)}, u32[]{:S(2)}) collective-permute-start(bf16[48,384]{1,0:T(8,128)(2,1)S(1)} %collective-permute-done.5), channel_id=1, source_target_pairs={{0,120},{8,0},{16,8},{24,16},{32,24},{40,32},{48,40},{56,48},{64,5... | collective-permute-start | bytes 110600 | tf_op jit(solution)/shard_map/ppermute | solution.py:26
  114.6 7.3 %collective-permute-start.6 = (bf16[48,384]{1,0:T(8,128)(2,1)S(1)}, bf16[48,384]{1,0:T(8,128)(2,1)S(1)}, u32[]{:S(2)}, u32[]{:S(2)}) collective-permute-start(bf16[48,384]{1,0:T(8,128)(2,1)S(1)} %collective-permute-done.4), channel_id=1, source_target_pairs={{0,8},{8,16},{16,24},{24,32},{32,40},{40,48},{48,56},{56,64},{64,7... | collective-permute-start | bytes 110600 | tf_op jit(solution)/shard_map/ppermute | solution.py:20
  116.2 7.3 %collective-permute-start.9 = (bf16[48,384]{1,0:T(8,128)(2,1)S(1)}, bf16[48,384]{1,0:T(8,128)(2,1)S(1)}, u32[]{:S(2)}, u32[]{:S(2)}) collective-permute-start(bf16[48,384]{1,0:T(8,128)(2,1)S(1)} %collective-permute-done.7), channel_id=1, source_target_pairs={{0,120},{8,0},{16,8},{24,16},{32,24},{40,32},{48,40},{56,48},{64,5... | collective-permute-start | bytes 110600 | tf_op jit(solution)/shard_map/ppermute | solution.py:26
  121.9 7.3 %collective-permute-start.8 = (bf16[48,384]{1,0:T(8,128)(2,1)S(1)}, bf16[48,384]{1,0:T(8,128)(2,1)S(1)}, u32[]{:S(2)}, u32[]{:S(2)}) collective-permute-start(bf16[48,384]{1,0:T(8,128)(2,1)S(1)} %collective-permute-done.6), channel_id=1, source_target_pairs={{0,8},{8,16},{16,24},{24,32},{32,40},{40,48},{48,56},{56,64},{64,7... | collective-permute-start | bytes 110600 | tf_op jit(solution)/shard_map/ppermute | solution.py:20
  123.5 7.3 %collective-permute-start.11 = (bf16[48,384]{1,0:T(8,128)(2,1)S(1)}, bf16[48,384]{1,0:T(8,128)(2,1)S(1)}, u32[]{:S(2)}, u32[]{:S(2)}) collective-permute-start(bf16[48,384]{1,0:T(8,128)(2,1)S(1)} %collective-permute-done.9), channel_id=1, source_target_pairs={{0,120},{8,0},{16,8},{24,16},{32,24},{40,32},{48,40},{56,48},{64,5... | collective-permute-start | bytes 110600 | tf_op jit(solution)/shard_map/ppermute | solution.py:26
  129.2 7.3 %collective-permute-start.10 = (bf16[48,384]{1,0:T(8,128)(2,1)S(1)}, bf16[48,384]{1,0:T(8,128)(2,1)S(1)}, u32[]{:S(2)}, u32[]{:S(2)}) collective-permute-start(bf16[48,384]{1,0:T(8,128)(2,1)S(1)} %collective-permute-done.8), channel_id=1, source_target_pairs={{0,8},{8,16},{16,24},{24,32},{32,40},{40,48},{48,56},{56,64},{64,7... | collective-permute-start | bytes 110600 | tf_op jit(solution)/shard_map/ppermute | solution.py:20
  130.8 13.5 %collective-permute-start.13 = (bf16[48,384]{1,0:T(8,128)(2,1)S(1)}, bf16[48,384]{1,0:T(8,128)(2,1)S(1)}, u32[]{:S(2)}, u32[]{:S(2)}) collective-permute-start(bf16[48,384]{1,0:T(8,128)(2,1)S(1)} %collective-permute-done.11), channel_id=1, source_target_pairs={{0,120},{8,0},{16,8},{24,16},{32,24},{40,32},{48,40},{56,48},{64,5... | collective-permute-start | bytes 110600 | tf_op jit(solution)/shard_map/ppermute | solution.py:26
  136.4 7.3 %collective-permute-start.12 = (bf16[48,384]{1,0:T(8,128)(2,1)S(1)}, bf16[48,384]{1,0:T(8,128)(2,1)S(1)}, u32[]{:S(2)}, u32[]{:S(2)}) collective-permute-start(bf16[48,384]{1,0:T(8,128)(2,1)S(1)} %collective-permute-done.10), channel_id=1, source_target_pairs={{0,8},{8,16},{16,24},{24,32},{32,40},{40,48},{48,56},{56,64},{64,7... | collective-permute-start | bytes 110600 | tf_op jit(solution)/shard_map/ppermute | solution.py:20
  143.7 7.3 %collective-permute-start.14 = (bf16[48,384]{1,0:T(8,128)(2,1)S(1)}, bf16[48,384]{1,0:T(8,128)(2,1)S(1)}, u32[]{:S(2)}, u32[]{:S(2)}) collective-permute-start(bf16[48,384]{1,0:T(8,128)(2,1)S(1)} %collective-permute-done.12), channel_id=1, source_target_pairs={{0,8},{8,16},{16,24},{24,32},{32,40},{40,48},{48,56},{56,64},{64,7... | collective-permute-start | bytes 110600 | tf_op jit(solution)/shard_map/ppermute | solution.py:20
  158.5 3.7 copy-start.21
  167.4 2.7 copy-start.8
  167.6 4.1 copy-start.15
  167.6 4.1 copy-start.18
  167.6 4.1 copy-start.19
  171.6 140.8 %all-reduce.4.cloned.1.call-start = ((), (), s32[]{:S(2)}) async-start(), calls=%async_computation.3 | async-start | bytes 3735552 | tf_op jit(solution)/shard_map/psum | solution.py:167
  174.4 5.0 %copy-start.12 = (bf16[256,384]{0,1:T(8,128)(2,1)S(1)}, bf16[256,384]{0,1:T(8,128)(2,1)}, u32[]{:S(2)}) copy-start(bf16[256,384]{0,1:T(8,128)(2,1)} %copy.86) | copy-start | bytes 589828
  174.4 5.1 %copy-start.13 = (bf16[256,384]{0,1:T(8,128)(2,1)S(1)}, bf16[256,384]{0,1:T(8,128)(2,1)}, u32[]{:S(2)}) copy-start(bf16[256,384]{0,1:T(8,128)(2,1)} %copy.85) | copy-start | bytes 589828
  242.8 3.1 copy-start.9
  247.5 182.9 %reduce-scatter.5.cloned.1.call-start = ((), (), s32[]{:S(2)}) async-start(), calls=%async_computation.4 | async-start | bytes 4423680 | tf_op jit(solution)/shard_map/reduce_scatter | solution.py:177
  371.0 8.9 %copy-start.23 = (bf16[3072,512]{1,0:T(8,128)(2,1)S(1)}, bf16[3072,512]{1,0:T(8,128)(2,1)}, u32[]{:S(2)}) copy-start(bf16[3072,512]{1,0:T(8,128)(2,1)} %param.33) | copy-start | bytes 9437188
  (10 other events, 20.1 us)
Sparse Core Ops, SparseCore 0:
  171.7 70.1 reduce-scatter.6
  247.7 64.6 all-reduce.3
  393.0 37.3 reduce-scatter.4
